TPU v7x, 32 devices: a whole 2x2x4 slice. The times are simulated.
32 devices in a mesh: groups: 2 (over y), cam: 4 (over z), tm: 2 (over x), chan: 2 (over core).
Axes of the slice: x: 2, y: 2, z: 4, core: 2. Of those that a mesh axis runs over, the one named last changes fastest.
Arguments:
- video: bfloat16 [16, 8, 16, 8, 256], P(('groups', 'cam'), 'tm', None, None, 'chan'), parts along dimension 0, may hold values from -6 to 6
- conv_weight: bfloat16 [27, 256, 256], P(None, None, 'chan'), may hold values from -0.078125 to 0.078125
- proj_weight: bfloat16 [256, 16], P('chan'), may hold values from -0.375 to 0.375
- rig_sizes: int32 [8], P('groups'), parts along dimension 0, may hold values from 1 to 3, as said below
- camera_order: int32 [16], P('groups'), parts along dimension 0, may hold values from 0 to 7, as said below
- owner_slot: int32 [8], P('groups'), parts along dimension 0, may hold values from 0 to 3, as said below
- cotangent: bfloat16 [8, 8, 16, 128], P(('groups', 'cam'), 'tm'), parts along dimension 0, may hold values from -6 to 6
Outputs:
- robot_latent: float32 [8, 8, 16, 128], P(('groups', 'cam'), 'tm'), parts along dimension 0
- grad_conv: bfloat16 [54, 256, 256], P('groups', None, 'chan'), parts along dimension 0
- grad_proj: float32 [512, 16], P(('groups', 'chan')), parts along dimension 0
- grad_video: bfloat16 [16, 8, 16, 8, 256], P(('groups', 'cam'), 'tm', None, None, 'chan'), parts along dimension 0
There are 2 independent parts, one for each index of `groups`. A program takes and returns all parts, laid end to end along the dimension named above; an argument that names none is the same for every part. Nothing has to cross between parts.
Inputs may be any that keep to these rules, and one draw needn't show every extreme that they name: `rig_sizes`: the sizes sum to 8; the largest is exactly 3. `camera_order`: A permutation; the cameras whose places fall from rig_sizes[0] + ... + rig_sizes[r-1] to below rig_sizes[0] + ... + rig_sizes[r] belong to robot r. `owner_slot`: A permutation of the output rows.
All inputs are finite; a program needn't handle non-finite values.
Results may differ from a plain program's by a relative error of at most 0.0059.
Values may be sent and summed in bfloat16 or wider, within the bound.
No kernel may reach another device: no remote copies, remote signals or barrier semaphores. Data moves between devices by JAX's collectives and lax.ppermute only.
A program may use at most 128 MiB of HBM per device.

v0:
```python
import jax
import jax.numpy as jnp
from jax import lax
from jax.sharding import PartitionSpec as P

KT = 3
KS = 3


def shifted(shard, axis, by):
    size = lax.axis_size(axis)
    pairs = [(i, i + by) for i in range(size) if 0 <= i + by < size]
    return lax.ppermute(shard, axis, pairs)


def tap_offsets():
    return [
        (shift_t, shift_h, shift_w)
        for shift_t in range(KT)
        for shift_h in range(KS)
        for shift_w in range(KS)
    ]


def forward_taps(extended, weight, frames, height, width):
    channels = extended.shape[-1]
    summed = jnp.zeros((extended.shape[0] * frames * height * width, weight.shape[2]), jnp.float32)
    for tap_index, (shift_t, shift_h, shift_w) in enumerate(tap_offsets()):
        window = extended[
            :, shift_t : shift_t + frames, shift_h : shift_h + height, shift_w : shift_w + width, :
        ].reshape(-1, channels)
        summed = summed + jnp.dot(window, weight[tap_index], preferred_element_type=jnp.float32)
    return summed


def weight_taps(extended, grad_rows, frames, height, width):
    channels = extended.shape[-1]
    results = []
    for shift_t, shift_h, shift_w in tap_offsets():
        window = extended[
            :, shift_t : shift_t + frames, shift_h : shift_h + height, shift_w : shift_w + width, :
        ].reshape(-1, channels)
        results.append(
            lax.dot_general(
                window, grad_rows, (((0,), (0,)), ((), ())), preferred_element_type=jnp.float32
            )
        )
    return jnp.stack(results)


def input_taps(grad_rows, weight, batch, frames, height, width):
    channels = weight.shape[1]
    pad_half = KS // 2
    padded = jnp.zeros(
        (batch, frames + KT - 1, height + KS - 1, width + KS - 1, channels), jnp.float32
    )
    for tap_index, (shift_t, shift_h, shift_w) in enumerate(tap_offsets()):
        backed = lax.dot_general(
            grad_rows,
            weight[tap_index],
            (((1,), (1,)), ((), ())),
            preferred_element_type=jnp.float32,
        )
        padded = padded.at[
            :, shift_t : shift_t + frames, shift_h : shift_h + height, shift_w : shift_w + width, :
        ].add(backed.reshape(batch, frames, height, width, channels))
    return padded[:, :, pad_half : pad_half + height, pad_half : pad_half + width, :]


def joining_matrix(rig_sizes, camera_order, owner_slot):
    robots = rig_sizes.shape[0]
    ends = jnp.cumsum(rig_sizes)
    robot_of = jnp.sum((ends[None, :] <= camera_order[:, None]).astype(jnp.int32), axis=1)
    member = robot_of[:, None] == jnp.arange(robots, dtype=jnp.int32)[None, :]
    slot_of = jnp.sum(jnp.where(member, owner_slot[None, :], 0), axis=1)
    count_of = jnp.sum(jnp.where(member, rig_sizes[None, :], 0), axis=1)
    share = 1.0 / count_of.astype(jnp.float32)
    placed = slot_of[None, :] == jnp.arange(robots, dtype=jnp.int32)[:, None]
    return jnp.where(placed, share[None, :], jnp.zeros_like(share)[None, :])


def body(video, conv_weight, proj_weight, rig_sizes, camera_order, owner_slot, cotangent):
    cam_dev, frames, height, width, half_chan = video.shape
    pad_half = KS // 2
    lat_width = proj_weight.shape[1]
    cache_half = shifted(video[:, frames - (KT - 1) :], "tm", 1)
    whole_now, whole_cache = (
        lax.all_gather(video, "chan", axis=4, tiled=True),
        lax.all_gather(cache_half, "chan", axis=4, tiled=True),
    )
    extended = jnp.concatenate([whole_cache, whole_now], axis=1)
    extended = jnp.pad(
        extended, ((0, 0), (0, 0), (pad_half, pad_half), (pad_half, pad_half), (0, 0))
    )
    pre = forward_taps(extended, conv_weight, frames, height, width)
    sigma = jax.nn.sigmoid(pre)
    act = (pre * sigma).astype(jnp.bfloat16)
    latent_part = jnp.dot(act, proj_weight, preferred_element_type=jnp.float32)
    latent = lax.psum(latent_part, "chan").astype(jnp.bfloat16)
    mixing = joining_matrix(rig_sizes, camera_order, owner_slot)
    cam_index = lax.axis_index("cam")
    my_row = lax.dynamic_slice_in_dim(mixing, cam_index, 1, 0)
    latent_maps = latent.reshape(cam_dev, frames, height, width * lat_width)
    block_in = lax.all_gather(latent_maps, "cam", axis=0, tiled=True)
    count_in = block_in.shape[0]
    flat_in = block_in.reshape(count_in, -1).astype(jnp.float32)
    added = jnp.dot(
        my_row, flat_in, precision=lax.Precision.HIGHEST, preferred_element_type=jnp.float32
    )
    robot_latent = added.reshape(
        jnp.zeros((1, frames, height, width * lat_width), jnp.float32).shape
    )
    my_cols = lax.dynamic_slice_in_dim(mixing, cam_index * cam_dev, cam_dev, 1)
    block_in = lax.all_gather(cotangent, "cam", axis=0, tiled=True)
    count_in = block_in.shape[0]
    flat_in = block_in.reshape(count_in, -1).astype(jnp.float32)
    spread = lax.dot_general(
        my_cols,
        flat_in,
        (((0,), (0,)), ((), ())),
        precision=lax.Precision.HIGHEST,
        preferred_element_type=jnp.float32,
    )
    dlatent = spread.astype(jnp.bfloat16).reshape(-1, lat_width)
    grad_proj_local = lax.dot_general(
        act, dlatent, (((0,), (0,)), ((), ())), preferred_element_type=jnp.float32
    )
    dact = lax.dot_general(
        dlatent, proj_weight, (((1,), (1,)), ((), ())), preferred_element_type=jnp.float32
    )
    dpre = (dact * sigma * (1.0 + pre * (1.0 - sigma))).astype(jnp.bfloat16)
    full_back = input_taps(dpre, conv_weight, cam_dev, frames, height, width)
    cache_part = full_back[:, : KT - 1]
    incoming = shifted(cache_part, "tm", -1)
    own_part = full_back[:, KT - 1 :]
    own_part = own_part.at[:, frames - (KT - 1) :].add(incoming)
    grad_conv_local = weight_taps(extended, dpre, frames, height, width)
    grad_conv, grad_proj = lax.psum((grad_conv_local, grad_proj_local), ("cam", "tm"))
    grad_video = lax.psum_scatter(
        own_part.astype(jnp.bfloat16), "chan", scatter_dimension=4, tiled=True
    )
    return (robot_latent, grad_conv.astype(jnp.bfloat16), grad_proj, grad_video)


def solution(mesh):
    return jax.shard_map(
        body,
        mesh=mesh,
        in_specs=(
            P(("groups", "cam"), "tm", None, None, "chan"),
            P(None, None, "chan"),
            P("chan", None),
            P("groups"),
            P("groups"),
            P("groups"),
            P(("groups", "cam"), "tm", None, None),
        ),
        out_specs=(
            P(("groups", "cam"), "tm", None, None),
            P("groups", None, "chan"),
            P(("groups", "chan"), None),
            P(("groups", "cam"), "tm", None, None, "chan"),
        ),
        check_vma=False,
    )
```

profile of v0, /device:TPU:0, one launch (start us, length us, event | category | flops | bytes accessed | tf_op | source)
XLA Modules:
  0.0 450.1 jit_solution(12302339504369722204)
XLA Ops:
  7.2 0.9 slice.1486
  8.2 4.8 %collective-permute-start = (bf16[2,2,16,8,128]{4,3,2,1,0:T(8,128)(2,1)S(1)}, bf16[2,2,16,8,128]{4,3,2,1,0:T(8,128)(2,1)S(1)}, u32[]{:S(2)}, u32[]{:S(2)}) collective-permute-start(bf16[2,2,16,8,128]{4,3,2,1,0:T(8,128)(2,1)S(1)} %slice.1486), channel_id=1, source_target_pairs={{0,2},{1,3},{4,6},{5,7},{8,10},{9,11},{12,14},{13,15},{16,18},{17,... | collective-permute-start | bytes 393224 | tf_op jit(solution)/shard_map/ppermute | solution.py:13
  13.0 0.8 reduce-window.8
  15.4 13.6 %all_gather.15 = bf16[4,4,16,128]{3,2,1,0:T(8,128)(2,1)S(1)} all-gather(bf16[1,4,16,128]{3,2,1,0:T(8,128)(2,1)} %param.69), channel_id=1, replica_groups=mesh['groups'=2,'cam'=4,'tm'=2,'chan'=2] {'cam'}, dimensions={0}, use_global_device_ids=true | all-gather | bytes 81920 | tf_op jit(solution)/shard_map/all_gather | solution.py:114
  30.2 2.4 all_gather.13
  32.5 2.0 all_gather.12
  35.0 2.3 pad_slice_fusion
  55.7 1.8 copy-done.3
  58.1 2.2 scatter-add.94
  60.3 6.7 %scatter-add.95 = f32[2,6,18,10,256]{4,3,2,1,0:T(8,128)} dynamic-update-slice(f32[2,6,18,10,256]{4,3,2,1,0:T(8,128)} %scatter-add.94, f32[2,4,16,8,256]{4,3,2,1,0:T(8,128)S(1)} %convolution_add_fusion.25, s32[]{:T(128)} %constant.917.clone.1, s32[]{:T(128)} %constant.917.clone.1, s32[]{:T(128)} %constant.917.clone.1, s32[]{:T(128)} %constant.926.clone.1, s32[]{:T(128)} %constant.917.clone.1) | dynamic-update-slice | bytes 2097156 | tf_op jit(solution)/shard_map/scatter-add | solution.py:66
  67.0 1.8 convolution_add_fusion.24
  68.9 6.7 %scatter-add.96 = f32[2,6,18,10,256]{4,3,2,1,0:T(8,128)} dynamic-update-slice(f32[2,6,18,10,256]{4,3,2,1,0:T(8,128)} %scatter-add.95, f32[2,4,16,8,256]{4,3,2,1,0:T(8,128)S(1)} %convolution_add_fusion.24, s32[]{:T(128)} %constant.917.clone.1, s32[]{:T(128)} %constant.917.clone.1, s32[]{:T(128)} %constant.917.clone.1, s32[]{:T(128)} %constant.924.clone.1, s32[]{:T(128)} %constant.917.clone.1) | dynamic-update-slice | bytes 2097156 | tf_op jit(solution)/shard_map/scatter-add | solution.py:66
  75.6 2.6 fusion.7
  78.1 1.8 convolution_add_fusion.22
  80.0 6.7 %scatter-add.100 = f32[2,6,18,10,256]{4,3,2,1,0:T(8,128)} dynamic-update-slice(f32[2,6,18,10,256]{4,3,2,1,0:T(8,128)} %fusion.7, f32[2,4,16,8,256]{4,3,2,1,0:T(8,128)S(1)} %convolution_add_fusion.22, s32[]{:T(128)} %constant.917.clone.1, s32[]{:T(128)} %constant.917.clone.1, s32[]{:T(128)} %constant.926.clone.1, s32[]{:T(128)} %constant.926.clone.1, s32[]{:T(128)} %constant.917.clone.1) | dynamic-update-slice | bytes 2097156 | tf_op jit(solution)/shard_map/scatter-add | solution.py:66
  86.7 3.8 convolution_add_fusion.21
  90.5 8.6 %scatter-add.101 = f32[2,6,18,10,256]{4,3,2,1,0:T(8,128)} dynamic-update-slice(f32[2,6,18,10,256]{4,3,2,1,0:T(8,128)} %scatter-add.100, f32[2,4,16,8,256]{4,3,2,1,0:T(8,128)S(1)} %convolution_add_fusion.21, s32[]{:T(128)} %constant.917.clone.1, s32[]{:T(128)} %bitcast.103, s32[]{:T(128)} %bitcast.104, s32[]{:T(128)} %bitcast.105, s32[]{:T(128)} %constant.917.clone.1) | dynamic-update-slice | bytes 2097156 | tf_op jit(solution)/shard_map/scatter-add | solution.py:66
  99.1 2.6 fusion.6
  101.8 1.9 convolution_add_fusion.19
  103.6 6.7 %scatter-add.105 = f32[2,6,18,10,256]{4,3,2,1,0:T(8,128)} dynamic-update-slice(f32[2,6,18,10,256]{4,3,2,1,0:T(8,128)} %fusion.6, f32[2,4,16,8,256]{4,3,2,1,0:T(8,128)S(1)} %convolution_add_fusion.19, s32[]{:T(128)} %constant.917.clone.1, s32[]{:T(128)} %constant.917.clone.1, s32[]{:T(128)} %constant.924.clone.1, s32[]{:T(128)} %constant.926.clone.1, s32[]{:T(128)} %constant.917.clone.1) | dynamic-update-slice | bytes 2097156 | tf_op jit(solution)/shard_map/scatter-add | solution.py:66
  110.3 1.9 convolution_add_fusion.18
  112.2 6.7 %scatter-add.106 = f32[2,6,18,10,256]{4,3,2,1,0:T(8,128)} dynamic-update-slice(f32[2,6,18,10,256]{4,3,2,1,0:T(8,128)} %scatter-add.105, f32[2,4,16,8,256]{4,3,2,1,0:T(8,128)S(1)} %convolution_add_fusion.18, s32[]{:T(128)} %constant.917.clone.1, s32[]{:T(128)} %constant.917.clone.1, s32[]{:T(128)} %constant.924.clone.1, s32[]{:T(128)} %constant.924.clone.1, s32[]{:T(128)} %constant.917.clone.1) | dynamic-update-slice | bytes 2097156 | tf_op jit(solution)/shard_map/scatter-add | solution.py:66
  118.9 2.7 fusion.5
  121.6 1.9 convolution_add_fusion.16
  123.4 6.8 %scatter-add.110 = f32[2,6,18,10,256]{4,3,2,1,0:T(8,128)} dynamic-update-slice(f32[2,6,18,10,256]{4,3,2,1,0:T(8,128)} %fusion.5, f32[2,4,16,8,256]{4,3,2,1,0:T(8,128)S(1)} %convolution_add_fusion.16, s32[]{:T(128)} %constant.917.clone.1, s32[]{:T(128)} %constant.926.clone.1, s32[]{:T(128)} %constant.917.clone.1, s32[]{:T(128)} %constant.926.clone.1, s32[]{:T(128)} %constant.917.clone.1) | dynamic-update-slice | bytes 2097156 | tf_op jit(solution)/shard_map/scatter-add | solution.py:66
  130.2 1.9 convolution_add_fusion.15
  132.1 6.8 %scatter-add.111 = f32[2,6,18,10,256]{4,3,2,1,0:T(8,128)} dynamic-update-slice(f32[2,6,18,10,256]{4,3,2,1,0:T(8,128)} %scatter-add.110, f32[2,4,16,8,256]{4,3,2,1,0:T(8,128)S(1)} %convolution_add_fusion.15, s32[]{:T(128)} %constant.917.clone.1, s32[]{:T(128)} %constant.926.clone.1, s32[]{:T(128)} %constant.917.clone.1, s32[]{:T(128)} %constant.924.clone.1, s32[]{:T(128)} %constant.917.clone.1) | dynamic-update-slice | bytes 2097156 | tf_op jit(solution)/shard_map/scatter-add | solution.py:66
  138.9 2.7 fusion.4
  141.5 1.9 convolution_add_fusion.13
  143.4 6.7 %scatter-add.115 = f32[2,6,18,10,256]{4,3,2,1,0:T(8,128)} dynamic-update-slice(f32[2,6,18,10,256]{4,3,2,1,0:T(8,128)} %fusion.4, f32[2,4,16,8,256]{4,3,2,1,0:T(8,128)S(1)} %convolution_add_fusion.13, s32[]{:T(128)} %constant.917.clone.1, s32[]{:T(128)} %constant.926.clone.1, s32[]{:T(128)} %constant.926.clone.1, s32[]{:T(128)} %constant.926.clone.1, s32[]{:T(128)} %constant.917.clone.1) | dynamic-update-slice | bytes 2097156 | tf_op jit(solution)/shard_map/scatter-add | solution.py:66
  150.1 1.9 convolution_add_fusion.12
  152.0 6.7 %scatter-add.116 = f32[2,6,18,10,256]{4,3,2,1,0:T(8,128)} dynamic-update-slice(f32[2,6,18,10,256]{4,3,2,1,0:T(8,128)} %scatter-add.115, f32[2,4,16,8,256]{4,3,2,1,0:T(8,128)S(1)} %convolution_add_fusion.12, s32[]{:T(128)} %constant.917.clone.1, s32[]{:T(128)} %constant.926.clone.1, s32[]{:T(128)} %constant.926.clone.1, s32[]{:T(128)} %constant.924.clone.1, s32[]{:T(128)} %constant.917.clone.1) | dynamic-update-slice | bytes 2097156 | tf_op jit(solution)/shard_map/scatter-add | solution.py:66
  158.8 2.7 fusion.3
  161.4 1.9 convolution_add_fusion.10
  163.3 6.7 %scatter-add.120 = f32[2,6,18,10,256]{4,3,2,1,0:T(8,128)} dynamic-update-slice(f32[2,6,18,10,256]{4,3,2,1,0:T(8,128)} %fusion.3, f32[2,4,16,8,256]{4,3,2,1,0:T(8,128)S(1)} %convolution_add_fusion.10, s32[]{:T(128)} %constant.917.clone.1, s32[]{:T(128)} %constant.926.clone.1, s32[]{:T(128)} %constant.924.clone.1, s32[]{:T(128)} %constant.926.clone.1, s32[]{:T(128)} %constant.917.clone.1) | dynamic-update-slice | bytes 2097156 | tf_op jit(solution)/shard_map/scatter-add | solution.py:66
  170.1 1.9 convolution_add_fusion.9
  172.0 6.7 %scatter-add.121 = f32[2,6,18,10,256]{4,3,2,1,0:T(8,128)} dynamic-update-slice(f32[2,6,18,10,256]{4,3,2,1,0:T(8,128)} %scatter-add.120, f32[2,4,16,8,256]{4,3,2,1,0:T(8,128)S(1)} %convolution_add_fusion.9, s32[]{:T(128)} %constant.917.clone.1, s32[]{:T(128)} %constant.926.clone.1, s32[]{:T(128)} %constant.924.clone.1, s32[]{:T(128)} %constant.924.clone.1, s32[]{:T(128)} %constant.917.clone.1) | dynamic-update-slice | bytes 2097156 | tf_op jit(solution)/shard_map/scatter-add | solution.py:66
  178.7 2.6 fusion.2
  181.3 1.9 convolution_add_fusion.7
  183.2 6.7 %scatter-add.125 = f32[2,6,18,10,256]{4,3,2,1,0:T(8,128)} dynamic-update-slice(f32[2,6,18,10,256]{4,3,2,1,0:T(8,128)} %fusion.2, f32[2,4,16,8,256]{4,3,2,1,0:T(8,128)S(1)} %convolution_add_fusion.7, s32[]{:T(128)} %constant.917.clone.1, s32[]{:T(128)} %constant.924.clone.1, s32[]{:T(128)} %constant.917.clone.1, s32[]{:T(128)} %constant.926.clone.1, s32[]{:T(128)} %constant.917.clone.1) | dynamic-update-slice | bytes 2097156 | tf_op jit(solution)/shard_map/scatter-add | solution.py:66
  189.9 1.9 convolution_add_fusion.6
  191.8 6.7 %scatter-add.126 = f32[2,6,18,10,256]{4,3,2,1,0:T(8,128)} dynamic-update-slice(f32[2,6,18,10,256]{4,3,2,1,0:T(8,128)} %scatter-add.125, f32[2,4,16,8,256]{4,3,2,1,0:T(8,128)S(1)} %convolution_add_fusion.6, s32[]{:T(128)} %constant.917.clone.1, s32[]{:T(128)} %constant.924.clone.1, s32[]{:T(128)} %constant.917.clone.1, s32[]{:T(128)} %constant.924.clone.1, s32[]{:T(128)} %constant.917.clone.1) | dynamic-update-slice | bytes 2097156 | tf_op jit(solution)/shard_map/scatter-add | solution.py:66
  198.5 2.6 fusion.1
  201.1 1.9 convolution_add_fusion.4
  203.0 7.0 %scatter-add.130 = f32[2,6,18,10,256]{4,3,2,1,0:T(8,128)} dynamic-update-slice(f32[2,6,18,10,256]{4,3,2,1,0:T(8,128)} %fusion.1, f32[2,4,16,8,256]{4,3,2,1,0:T(8,128)S(1)} %convolution_add_fusion.4, s32[]{:T(128)} %constant.917.clone.1, s32[]{:T(128)} %constant.924.clone.1, s32[]{:T(128)} %constant.926.clone.1, s32[]{:T(128)} %constant.926.clone.1, s32[]{:T(128)} %constant.917.clone.1) | dynamic-update-slice | bytes 2097156 | tf_op jit(solution)/shard_map/scatter-add | solution.py:66
  210.0 1.9 convolution_add_fusion.3
  211.9 6.7 %scatter-add.131 = f32[2,6,18,10,256]{4,3,2,1,0:T(8,128)} dynamic-update-slice(f32[2,6,18,10,256]{4,3,2,1,0:T(8,128)} %scatter-add.130, f32[2,4,16,8,256]{4,3,2,1,0:T(8,128)S(1)} %convolution_add_fusion.3, s32[]{:T(128)} %constant.917.clone.1, s32[]{:T(128)} %constant.924.clone.1, s32[]{:T(128)} %constant.926.clone.1, s32[]{:T(128)} %constant.924.clone.1, s32[]{:T(128)} %constant.917.clone.1) | dynamic-update-slice | bytes 2097156 | tf_op jit(solution)/shard_map/scatter-add | solution.py:66
  218.6 2.6 fusion
  221.2 1.9 convolution_add_fusion.1
  223.1 6.7 %scatter-add.135 = f32[2,6,18,10,256]{4,3,2,1,0:T(8,128)} dynamic-update-slice(f32[2,6,18,10,256]{4,3,2,1,0:T(8,128)} %fusion, f32[2,4,16,8,256]{4,3,2,1,0:T(8,128)S(1)} %convolution_add_fusion.1, s32[]{:T(128)} %constant.917.clone.1, s32[]{:T(128)} %constant.924.clone.1, s32[]{:T(128)} %constant.924.clone.1, s32[]{:T(128)} %constant.926.clone.1, s32[]{:T(128)} %constant.917.clone.1) | dynamic-update-slice | bytes 2097156 | tf_op jit(solution)/shard_map/scatter-add | solution.py:66
  229.8 1.9 convolution_add_fusion
  231.7 6.7 %scatter-add.136 = f32[2,6,18,10,256]{4,3,2,1,0:T(8,128)} dynamic-update-slice(f32[2,6,18,10,256]{4,3,2,1,0:T(8,128)} %scatter-add.135, f32[2,4,16,8,256]{4,3,2,1,0:T(8,128)S(1)} %convolution_add_fusion, s32[]{:T(128)} %constant.917.clone.1, s32[]{:T(128)} %constant.924.clone.1, s32[]{:T(128)} %constant.924.clone.1, s32[]{:T(128)} %constant.924.clone.1, s32[]{:T(128)} %constant.917.clone.1) | dynamic-update-slice | bytes 2097156 | tf_op jit(solution)/shard_map/scatter-add | solution.py:66
  238.4 1.3 slice.1599
  239.6 1.3 collective-permute-start.1
  240.9 3.6 psum.21
  244.6 1.7 slice.1597
  246.6 13.4 %all_gather.14 = bf16[8,4,16,128]{3,2,1,0:T(8,128)(2,1)S(1)} all-gather(bf16[2,4,16,128]{3,2,1,0:T(8,128)(2,1)S(1)} %reshape.1490), channel_id=1, replica_groups=mesh['groups'=2,'cam'=4,'tm'=2,'chan'=2] {'cam'}, dimensions={0}, use_global_device_ids=true | all-gather | bytes 163840 | tf_op jit(solution)/shard_map/all_gather | solution.py:104
  260.1 0.9 fusion.152
  261.2 1.4 fusion.37
  262.5 11.8 %copy.48 = bf16[2,4,16,8,256]{3,2,1,0,4:T(8,128)(2,1)} copy(bf16[2,4,16,8,256]{4,3,2,1,0:T(8,128)(2,1)S(1)} %fusion.37) | data formatting | bytes 1048576
  274.3 13.6 %reshape.1527 = bf16[256,1024]{1,0:T(8,128)(2,1)} reshape(bf16[256,2,4,16,8]{4,3,2,1,0:T(8,128)(2,1)} %bitcast.557) | data formatting | bytes 1048576
  288.0 142.3 %all-reduce.4 = (bf16[27,256,128]{2,1,0:T(8,128)(2,1)}, f32[128,16]{0,1:T(8,128)}) all-reduce(f32[27,256,128]{2,1,0:T(8,128)S(1)} %copy-done.4, f32[128,16]{0,1:T(8,128)S(1)} %fusion.156), channel_id=1, replica_groups=mesh['groups'=2,'cam'=4,'tm'=2,'chan'=2] {'cam','tm'}, use_global_device_ids=true, to_apply=%region_5.6 | all-reduce | flops 886784 | bytes 5324800 | tf_op jit(solution)/shard_map/psum | solution.py:138
  430.3 6.8 %reshape.1528 = bf16[128,2,4,16,8]{4,3,2,1,0:T(8,128)(2,1)} reshape(bf16[128,1024]{1,0:T(8,128)(2,1)} %reduce-scatter.4.cloned.1.call-done) | data formatting | bytes 524288
  437.2 6.1 %copy.49 = bf16[2,4,16,8,128]{4,3,2,1,0:T(8,128)(2,1)} copy(bf16[2,4,16,8,128]{3,2,1,0,4:T(8,128)(2,1)} %bitcast.558) | data formatting | bytes 524288
  (91 shorter events, 22.6 us)
Async XLA Ops:
  7.2 38.4 %copy-start = (bf16[128,16]{0,1:T(8,128)(2,1)S(1)}, bf16[128,16]{0,1:T(8,128)(2,1)}, u32[]{:S(2)}) copy-start(bf16[128,16]{0,1:T(8,128)(2,1)} %param.65) | copy-start | bytes 12292
  7.2 423.2 %reduce-scatter.4.cloned.1.call-start = ((), (), s32[]{:S(2)}) async-start(), calls=%async_computation.1 | async-start | bytes 786432
  8.2 24.4 %collective-permute-start = (bf16[2,2,16,8,128]{4,3,2,1,0:T(8,128)(2,1)S(1)}, bf16[2,2,16,8,128]{4,3,2,1,0:T(8,128)(2,1)S(1)}, u32[]{:S(2)}, u32[]{:S(2)}) collective-permute-start(bf16[2,2,16,8,128]{4,3,2,1,0:T(8,128)(2,1)S(1)} %slice.1486), channel_id=1, source_target_pairs={{0,2},{1,3},{4,6},{5,7},{8,10},{9,11},{12,14},{13,15},{16,18},{17,... | collective-permute-start | bytes 393224 | tf_op jit(solution)/shard_map/ppermute | solution.py:13
  35.0 2.3 copy-start.2
  45.6 2.2 copy-start.5
  55.7 1.8 copy-start.3
  229.8 31.2 %copy-start.6 = (bf16[1024,128]{1,0:T(8,128)(2,1)S(1)}, bf16[1024,128]{1,0:T(8,128)(2,1)}, u32[]{:S(2)}) copy-start(bf16[1024,128]{1,0:T(8,128)(2,1)} %copy-done.5) | copy-start | bytes 786436
  239.6 21.5 %collective-permute-start.1 = (f32[2,2,16,8,256]{4,3,2,1,0:T(8,128)S(1)}, f32[2,2,16,8,256]{4,3,2,1,0:T(8,128)S(1)}, u32[]{:S(2)}, u32[]{:S(2)}) collective-permute-start(f32[2,2,16,8,256]{4,3,2,1,0:T(8,128)S(1)} %slice.1599), channel_id=1, source_target_pairs={{2,0},{3,1},{6,4},{7,5},{10,8},{11,9},{14,12},{15,13},{18,16},{19,... | collective-permute-start | bytes 1572872 | tf_op jit(solution)/shard_map/ppermute | solution.py:13
  274.3 13.7 %copy-start.4 = (f32[27,256,128]{2,1,0:T(8,128)S(1)}, f32[27,256,128]{2,1,0:T(8,128)}, u32[]{:S(2)}) copy-start(f32[27,256,128]{2,1,0:T(8,128)} %copy-done.3) | copy-start | bytes 10616836
  288.0 155.3 %copy-start.1 = (bf16[128,16]{0,1:T(8,128)(2,1)S(1)}, bf16[128,16]{0,1:T(8,128)(2,1)}, u32[]{:S(2)}) copy-start(bf16[128,16]{0,1:T(8,128)(2,1)} %param.65) | copy-start | bytes 12292
Sparse Core Ops, SparseCore 0:
  288.1 10.2 reduce-scatter.3
where the time goes:
time: 454 us; the launch traced here: 450 us
  blocking collectives  177 us (39%)
  local copies, waits for them, and re-layouts  173 us (38%)
  matrix products  74.9 us (16%)
  between operations  14.6 us (3%)
  starting transfers between devices  6.18 us (1%)
    psum x1, blocking collectives, body(): lax.psum((grad_conv_local, grad_proj_local), ('cam', 'tm'))  142 us
    scatter-add x19, local copies, waits for them, and re-layouts, input_taps(): padded = padded.at[:, shift_t:shift_t + frames, shift_h:shift_h + height,...  125 us
    dot_general x27, matrix products, input_taps(): lax.dot_general(grad_rows, weight[tap_index], (((1,), (1,)), ((), ())), p...  55.4 us
    unnamed x20, local copies, waits for them, and re-layouts  40.4 us
    all_gather x1, blocking collectives, body(): block_in = lax.all_gather(cotangent, 'cam', axis=0, tiled=True)  13.6 us
    all_gather x1, blocking collectives, body(): block_in = lax.all_gather(latent_maps, 'cam', axis=0, tiled=True)  13.4 us
    dot_general x27, matrix products, weight_taps(): lax.dot_general(window, grad_rows, (((0,), (0,)), ((), ())), preferred_el...  9.49 us
  transfers between devices with their start and end apart: 3, of which 0 were waited for; matrix products, arithmetic and copies ran while one was open for 2% of the time, Pallas kernels for 0%

commit v1 on v0

--- a/solution.py
+++ b/solution.py
@@ -5,6 +5,18 @@
 
 KT = 3
 KS = 3
+
+
+def gather_by_bits(x, axis, dim):
+    ways, here = (lax.axis_size(axis), lax.axis_index(axis))
+    grown, reach = (x, 1)
+    while reach < ways:
+        theirs = lax.ppermute(grown, axis, [(d, d ^ reach) for d in range(ways)])
+        mine_first = jnp.concatenate([grown, theirs], axis=dim)
+        theirs_first = jnp.concatenate([theirs, grown], axis=dim)
+        grown = jnp.where(here & reach == 0, mine_first, theirs_first)
+        reach = 2 * reach
+    return grown
 
 
 def shifted(shard, axis, by):
@@ -101,7 +113,7 @@
     cam_index = lax.axis_index("cam")
     my_row = lax.dynamic_slice_in_dim(mixing, cam_index, 1, 0)
     latent_maps = latent.reshape(cam_dev, frames, height, width * lat_width)
-    block_in = lax.all_gather(latent_maps, "cam", axis=0, tiled=True)
+    block_in = gather_by_bits(latent_maps, "cam", 0)
     count_in = block_in.shape[0]
     flat_in = block_in.reshape(count_in, -1).astype(jnp.float32)
     added = jnp.dot(

time: 454 us -> 481 us (1.059); the launches traced: 450 us -> 472 us
  waiting for transfers between devices: 0.02 us -> 10.9 us
  matrix products: 74.9 us -> 82.7 us
    all_gather x1 -> x0, blocking collectives: 13.4 us -> none  [body(): block_in = lax.all_gather(latent_maps, 'cam', axis=0, tiled=True)]
    psum x1, blocking collectives: 142 us -> 152 us  [body(): lax.psum((grad_conv_local, grad_proj_local), ('cam', 'tm'))]
    unnamed x2, waiting for transfers between devices: 0.02 us -> 7.24 us
    unnamed x20 -> x111, local copies, waits for them, and re-layouts: 40.4 us -> 41.2 us
  transfers between devices with their start and end apart: 3 -> 5, of which waited for: 0 -> 2; matrix products, arithmetic and copies ran while one was open for 2% -> 44% of each run, Pallas kernels for 0% -> 0%
where the time goes in v1:
time: 481 us; the launch traced here: 472 us
  local copies, waits for them, and re-layouts  175 us (36%)
  blocking collectives  174 us (36%)
  matrix products  82.7 us (17%)
  between operations  15.5 us (3%)
  waiting for transfers between devices  10.9 us (2%)
  starting transfers between devices  9.4 us (2%)
    psum x1, blocking collectives, body(): lax.psum((grad_conv_local, grad_proj_local), ('cam', 'tm'))  152 us
    scatter-add x19, local copies, waits for them, and re-layouts, input_taps(): padded = padded.at[:, shift_t:shift_t + frames, shift_h:shift_h + height,...  126 us
    dot_general x27, matrix products, input_taps(): lax.dot_general(grad_rows, weight[tap_index], (((1,), (1,)), ((), ())), p...  56.2 us
    unnamed x111, local copies, waits for them, and re-layouts  41.2 us
    all_gather x1, blocking collectives, body(): block_in = lax.all_gather(cotangent, 'cam', axis=0, tiled=True)  13.6 us
    dot_general x27, matrix products, weight_taps(): lax.dot_general(window, grad_rows, (((0,), (0,)), ((), ())), preferred_el...  13.5 us
  transfers between devices with their start and end apart: 5, of which 2 were waited for; matrix products, arithmetic and copies ran while one was open for 44% of the time, Pallas kernels for 0%

profile of v1, /device:TPU:0, one launch (start us, length us, event | category | flops | bytes accessed | tf_op | source)
XLA Modules:
  0.0 471.6 jit_solution(12707462941861025695)
XLA Ops:
  8.2 4.8 %collective-permute-start = (bf16[2,2,16,8,128]{4,3,2,1,0:T(8,128)(2,1)S(1)}, bf16[2,2,16,8,128]{4,3,2,1,0:T(8,128)(2,1)S(1)}, u32[]{:S(2)}, u32[]{:S(2)}) collective-permute-start(bf16[2,2,16,8,128]{4,3,2,1,0:T(8,128)(2,1)S(1)} %slice.1486), channel_id=1, source_target_pairs={{0,2},{1,3},{4,6},{5,7},{8,10},{9,11},{12,14},{13,15},{16,18},{17,... | collective-permute-start | bytes 393224 | tf_op jit(solution)/shard_map/ppermute | solution.py:25
  15.4 13.6 %all_gather.11 = bf16[4,4,16,128]{3,2,1,0:T(8,128)(2,1)S(1)} all-gather(bf16[1,4,16,128]{3,2,1,0:T(8,128)(2,1)} %param.69), channel_id=1, replica_groups=mesh['groups'=2,'cam'=4,'tm'=2,'chan'=2] {'cam'}, dimensions={0}, use_global_device_ids=true | all-gather | bytes 81920 | tf_op jit(solution)/shard_map/all_gather | solution.py:126
  30.2 2.4 all_gather.10
  32.6 2.0 all_gather.9
  35.1 2.1 pad_slice_fusion
  47.7 4.1 psum.21
  52.2 1.6 collective-permute-start.1
  55.0 1.5 fusion.9
  56.5 1.5 fusion.36
  58.0 1.4 fusion.35
  70.5 1.7 copy-done.47
  73.8 2.3 scatter-add.94
  76.1 7.2 %scatter-add.95 = f32[2,6,18,10,256]{4,3,2,1,0:T(8,128)} dynamic-update-slice(f32[2,6,18,10,256]{4,3,2,1,0:T(8,128)} %scatter-add.94, f32[2,4,16,8,256]{4,3,2,1,0:T(8,128)} %convolution_add_fusion.25, s32[]{:T(128)} %constant.918.clone.1, s32[]{:T(128)} %constant.918.clone.1, s32[]{:T(128)} %constant.918.clone.1, s32[]{:T(128)} %constant.925.clone.1, s32[]{:T(128)} %constant.918.clone.1) | dynamic-update-slice | bytes 2097156 | tf_op jit(solution)/shard_map/scatter-add | solution.py:78
  83.3 1.8 convolution_add_fusion.24
  85.2 6.7 %scatter-add.96 = f32[2,6,18,10,256]{4,3,2,1,0:T(8,128)} dynamic-update-slice(f32[2,6,18,10,256]{4,3,2,1,0:T(8,128)} %scatter-add.95, f32[2,4,16,8,256]{4,3,2,1,0:T(8,128)S(1)} %convolution_add_fusion.24, s32[]{:T(128)} %constant.918.clone.1, s32[]{:T(128)} %constant.918.clone.1, s32[]{:T(128)} %constant.918.clone.1, s32[]{:T(128)} %constant.924.clone.1, s32[]{:T(128)} %constant.918.clone.1) | dynamic-update-slice | bytes 2097156 | tf_op jit(solution)/shard_map/scatter-add | solution.py:78
  91.9 2.6 fusion.7
  94.5 1.8 convolution_add_fusion.22
  96.3 6.7 %scatter-add.100 = f32[2,6,18,10,256]{4,3,2,1,0:T(8,128)} dynamic-update-slice(f32[2,6,18,10,256]{4,3,2,1,0:T(8,128)} %fusion.7, f32[2,4,16,8,256]{4,3,2,1,0:T(8,128)S(1)} %convolution_add_fusion.22, s32[]{:T(128)} %constant.918.clone.1, s32[]{:T(128)} %constant.918.clone.1, s32[]{:T(128)} %constant.925.clone.1, s32[]{:T(128)} %constant.925.clone.1, s32[]{:T(128)} %constant.918.clone.1) | dynamic-update-slice | bytes 2097156 | tf_op jit(solution)/shard_map/scatter-add | solution.py:78
  103.1 3.8 convolution_add_fusion.21
  106.9 8.7 %scatter-add.101 = f32[2,6,18,10,256]{4,3,2,1,0:T(8,128)} dynamic-update-slice(f32[2,6,18,10,256]{4,3,2,1,0:T(8,128)} %scatter-add.100, f32[2,4,16,8,256]{4,3,2,1,0:T(8,128)S(1)} %convolution_add_fusion.21, s32[]{:T(128)} %constant.918.clone.1, s32[]{:T(128)} %bitcast.103, s32[]{:T(128)} %bitcast.104, s32[]{:T(128)} %bitcast.105, s32[]{:T(128)} %constant.918.clone.1) | dynamic-update-slice | bytes 2097156 | tf_op jit(solution)/shard_map/scatter-add | solution.py:78
  115.5 2.6 fusion.6
  118.1 1.9 convolution_add_fusion.19
  120.0 6.7 %scatter-add.105 = f32[2,6,18,10,256]{4,3,2,1,0:T(8,128)} dynamic-update-slice(f32[2,6,18,10,256]{4,3,2,1,0:T(8,128)} %fusion.6, f32[2,4,16,8,256]{4,3,2,1,0:T(8,128)S(1)} %convolution_add_fusion.19, s32[]{:T(128)} %constant.918.clone.1, s32[]{:T(128)} %constant.918.clone.1, s32[]{:T(128)} %constant.924.clone.1, s32[]{:T(128)} %constant.925.clone.1, s32[]{:T(128)} %constant.918.clone.1) | dynamic-update-slice | bytes 2097156 | tf_op jit(solution)/shard_map/scatter-add | solution.py:78
  126.7 1.9 convolution_add_fusion.18
  128.6 6.7 %scatter-add.106 = f32[2,6,18,10,256]{4,3,2,1,0:T(8,128)} dynamic-update-slice(f32[2,6,18,10,256]{4,3,2,1,0:T(8,128)} %scatter-add.105, f32[2,4,16,8,256]{4,3,2,1,0:T(8,128)S(1)} %convolution_add_fusion.18, s32[]{:T(128)} %constant.918.clone.1, s32[]{:T(128)} %constant.918.clone.1, s32[]{:T(128)} %constant.924.clone.1, s32[]{:T(128)} %constant.924.clone.1, s32[]{:T(128)} %constant.918.clone.1) | dynamic-update-slice | bytes 2097156 | tf_op jit(solution)/shard_map/scatter-add | solution.py:78
  135.3 2.6 fusion.5
  138.0 1.9 convolution_add_fusion.16
  139.9 6.7 %scatter-add.110 = f32[2,6,18,10,256]{4,3,2,1,0:T(8,128)} dynamic-update-slice(f32[2,6,18,10,256]{4,3,2,1,0:T(8,128)} %fusion.5, f32[2,4,16,8,256]{4,3,2,1,0:T(8,128)S(1)} %convolution_add_fusion.16, s32[]{:T(128)} %constant.918.clone.1, s32[]{:T(128)} %constant.925.clone.1, s32[]{:T(128)} %constant.918.clone.1, s32[]{:T(128)} %constant.925.clone.1, s32[]{:T(128)} %constant.918.clone.1) | dynamic-update-slice | bytes 2097156 | tf_op jit(solution)/shard_map/scatter-add | solution.py:78
  146.6 1.9 convolution_add_fusion.15
  148.5 6.7 %scatter-add.111 = f32[2,6,18,10,256]{4,3,2,1,0:T(8,128)} dynamic-update-slice(f32[2,6,18,10,256]{4,3,2,1,0:T(8,128)} %scatter-add.110, f32[2,4,16,8,256]{4,3,2,1,0:T(8,128)S(1)} %convolution_add_fusion.15, s32[]{:T(128)} %constant.918.clone.1, s32[]{:T(128)} %constant.925.clone.1, s32[]{:T(128)} %constant.918.clone.1, s32[]{:T(128)} %constant.924.clone.1, s32[]{:T(128)} %constant.918.clone.1) | dynamic-update-slice | bytes 2097156 | tf_op jit(solution)/shard_map/scatter-add | solution.py:78
  155.3 2.6 fusion.4
  157.9 1.9 convolution_add_fusion.13
  159.8 6.7 %scatter-add.115 = f32[2,6,18,10,256]{4,3,2,1,0:T(8,128)} dynamic-update-slice(f32[2,6,18,10,256]{4,3,2,1,0:T(8,128)} %fusion.4, f32[2,4,16,8,256]{4,3,2,1,0:T(8,128)S(1)} %convolution_add_fusion.13, s32[]{:T(128)} %constant.918.clone.1, s32[]{:T(128)} %constant.925.clone.1, s32[]{:T(128)} %constant.925.clone.1, s32[]{:T(128)} %constant.925.clone.1, s32[]{:T(128)} %constant.918.clone.1) | dynamic-update-slice | bytes 2097156 | tf_op jit(solution)/shard_map/scatter-add | solution.py:78
  166.5 1.9 convolution_add_fusion.12
  168.4 6.7 %scatter-add.116 = f32[2,6,18,10,256]{4,3,2,1,0:T(8,128)} dynamic-update-slice(f32[2,6,18,10,256]{4,3,2,1,0:T(8,128)} %scatter-add.115, f32[2,4,16,8,256]{4,3,2,1,0:T(8,128)S(1)} %convolution_add_fusion.12, s32[]{:T(128)} %constant.918.clone.1, s32[]{:T(128)} %constant.925.clone.1, s32[]{:T(128)} %constant.925.clone.1, s32[]{:T(128)} %constant.924.clone.1, s32[]{:T(128)} %constant.918.clone.1) | dynamic-update-slice | bytes 2097156 | tf_op jit(solution)/shard_map/scatter-add | solution.py:78
  175.1 2.6 fusion.3
  177.7 1.9 convolution_add_fusion.10
  179.6 6.7 %scatter-add.120 = f32[2,6,18,10,256]{4,3,2,1,0:T(8,128)} dynamic-update-slice(f32[2,6,18,10,256]{4,3,2,1,0:T(8,128)} %fusion.3, f32[2,4,16,8,256]{4,3,2,1,0:T(8,128)S(1)} %convolution_add_fusion.10, s32[]{:T(128)} %constant.918.clone.1, s32[]{:T(128)} %constant.925.clone.1, s32[]{:T(128)} %constant.924.clone.1, s32[]{:T(128)} %constant.925.clone.1, s32[]{:T(128)} %constant.918.clone.1) | dynamic-update-slice | bytes 2097156 | tf_op jit(solution)/shard_map/scatter-add | solution.py:78
  186.3 1.9 convolution_add_fusion.9
  188.2 6.7 %scatter-add.121 = f32[2,6,18,10,256]{4,3,2,1,0:T(8,128)} dynamic-update-slice(f32[2,6,18,10,256]{4,3,2,1,0:T(8,128)} %scatter-add.120, f32[2,4,16,8,256]{4,3,2,1,0:T(8,128)S(1)} %convolution_add_fusion.9, s32[]{:T(128)} %constant.918.clone.1, s32[]{:T(128)} %constant.925.clone.1, s32[]{:T(128)} %constant.924.clone.1, s32[]{:T(128)} %constant.924.clone.1, s32[]{:T(128)} %constant.918.clone.1) | dynamic-update-slice | bytes 2097156 | tf_op jit(solution)/shard_map/scatter-add | solution.py:78
  194.9 2.6 fusion.2
  197.5 1.9 convolution_add_fusion.7
  199.4 6.7 %scatter-add.125 = f32[2,6,18,10,256]{4,3,2,1,0:T(8,128)} dynamic-update-slice(f32[2,6,18,10,256]{4,3,2,1,0:T(8,128)} %fusion.2, f32[2,4,16,8,256]{4,3,2,1,0:T(8,128)S(1)} %convolution_add_fusion.7, s32[]{:T(128)} %constant.918.clone.1, s32[]{:T(128)} %constant.924.clone.1, s32[]{:T(128)} %constant.918.clone.1, s32[]{:T(128)} %constant.925.clone.1, s32[]{:T(128)} %constant.918.clone.1) | dynamic-update-slice | bytes 2097156 | tf_op jit(solution)/shard_map/scatter-add | solution.py:78
  206.2 1.9 convolution_add_fusion.6
  208.0 6.7 %scatter-add.126 = f32[2,6,18,10,256]{4,3,2,1,0:T(8,128)} dynamic-update-slice(f32[2,6,18,10,256]{4,3,2,1,0:T(8,128)} %scatter-add.125, f32[2,4,16,8,256]{4,3,2,1,0:T(8,128)S(1)} %convolution_add_fusion.6, s32[]{:T(128)} %constant.918.clone.1, s32[]{:T(128)} %constant.924.clone.1, s32[]{:T(128)} %constant.918.clone.1, s32[]{:T(128)} %constant.924.clone.1, s32[]{:T(128)} %constant.918.clone.1) | dynamic-update-slice | bytes 2097156 | tf_op jit(solution)/shard_map/scatter-add | solution.py:78
  214.8 2.6 fusion.1
  217.3 1.9 convolution_add_fusion.4
  219.2 6.7 %scatter-add.130 = f32[2,6,18,10,256]{4,3,2,1,0:T(8,128)} dynamic-update-slice(f32[2,6,18,10,256]{4,3,2,1,0:T(8,128)} %fusion.1, f32[2,4,16,8,256]{4,3,2,1,0:T(8,128)S(1)} %convolution_add_fusion.4, s32[]{:T(128)} %constant.918.clone.1, s32[]{:T(128)} %constant.924.clone.1, s32[]{:T(128)} %constant.925.clone.1, s32[]{:T(128)} %constant.925.clone.1, s32[]{:T(128)} %constant.918.clone.1) | dynamic-update-slice | bytes 2097156 | tf_op jit(solution)/shard_map/scatter-add | solution.py:78
  225.9 1.9 convolution_add_fusion.3
  227.8 6.7 %scatter-add.131 = f32[2,6,18,10,256]{4,3,2,1,0:T(8,128)} dynamic-update-slice(f32[2,6,18,10,256]{4,3,2,1,0:T(8,128)} %scatter-add.130, f32[2,4,16,8,256]{4,3,2,1,0:T(8,128)S(1)} %convolution_add_fusion.3, s32[]{:T(128)} %constant.918.clone.1, s32[]{:T(128)} %constant.924.clone.1, s32[]{:T(128)} %constant.925.clone.1, s32[]{:T(128)} %constant.924.clone.1, s32[]{:T(128)} %constant.918.clone.1) | dynamic-update-slice | bytes 2097156 | tf_op jit(solution)/shard_map/scatter-add | solution.py:78
  234.5 2.6 fusion
  237.1 1.9 convolution_add_fusion.1
  239.0 6.7 %scatter-add.135 = f32[2,6,18,10,256]{4,3,2,1,0:T(8,128)} dynamic-update-slice(f32[2,6,18,10,256]{4,3,2,1,0:T(8,128)} %fusion, f32[2,4,16,8,256]{4,3,2,1,0:T(8,128)S(1)} %convolution_add_fusion.1, s32[]{:T(128)} %constant.918.clone.1, s32[]{:T(128)} %constant.924.clone.1, s32[]{:T(128)} %constant.924.clone.1, s32[]{:T(128)} %constant.925.clone.1, s32[]{:T(128)} %constant.918.clone.1) | dynamic-update-slice | bytes 2097156 | tf_op jit(solution)/shard_map/scatter-add | solution.py:78
  245.7 1.9 convolution_add_fusion
  247.6 6.9 %scatter-add.136 = f32[2,6,18,10,256]{4,3,2,1,0:T(8,128)} dynamic-update-slice(f32[2,6,18,10,256]{4,3,2,1,0:T(8,128)} %scatter-add.135, f32[2,4,16,8,256]{4,3,2,1,0:T(8,128)S(1)} %convolution_add_fusion, s32[]{:T(128)} %constant.918.clone.1, s32[]{:T(128)} %constant.924.clone.1, s32[]{:T(128)} %constant.924.clone.1, s32[]{:T(128)} %constant.924.clone.1, s32[]{:T(128)} %constant.918.clone.1) | dynamic-update-slice | bytes 2097156 | tf_op jit(solution)/shard_map/scatter-add | solution.py:78
  257.1 152.1 %all-reduce.4 = (bf16[27,256,128]{2,1,0:T(8,128)(2,1)}, f32[128,16]{0,1:T(8,128)}) all-reduce(f32[27,256,128]{2,1,0:T(8,128)} %copy-done.47, f32[128,16]{0,1:T(8,128)S(1)} %fusion.156), channel_id=1, replica_groups=mesh['groups'=2,'cam'=4,'tm'=2,'chan'=2] {'cam','tm'}, use_global_device_ids=true, to_apply=%region_5.6 | all-reduce | flops 886784 | bytes 5324800 | tf_op jit(solution)/shard_map/psum | solution.py:150
  409.4 1.7 slice.1597
  411.1 1.6 collective-permute-start.2
  412.9 3.7 collective-permute-done.2
  418.0 11.8 %copy.51 = bf16[2,4,16,8,256]{3,2,1,0,4:T(8,128)(2,1)} copy(bf16[2,4,16,8,256]{4,3,2,1,0:T(8,128)(2,1)S(1)} %fusion.37) | data formatting | bytes 1048576
  429.8 13.5 %reshape.1534 = bf16[256,1024]{1,0:T(8,128)(2,1)} reshape(bf16[256,2,4,16,8]{4,3,2,1,0:T(8,128)(2,1)} %bitcast.562) | data formatting | bytes 1048576
  444.3 7.2 %reduce-scatter.4.cloned.1.call-done = bf16[128,1024]{1,0:T(8,128)(2,1)} async-done(((bf16[256,1024]{1,0:T(8,128)(2,1)}), bf16[128,1024]{1,0:T(8,128)(2,1)}) %reduce-scatter.4.cloned.1.call-update) | async-done | bytes 262160
  451.5 6.8 %reshape.1535 = bf16[128,2,4,16,8]{4,3,2,1,0:T(8,128)(2,1)} reshape(bf16[128,1024]{1,0:T(8,128)(2,1)} %reduce-scatter.4.cloned.1.call-done) | data formatting | bytes 524288
  458.4 6.1 %copy.52 = bf16[2,4,16,8,128]{4,3,2,1,0:T(8,128)(2,1)} copy(bf16[2,4,16,8,128]{3,2,1,0,4:T(8,128)(2,1)} %bitcast.563) | data formatting | bytes 524288
  (189 shorter events, 34.3 us)
Async XLA Ops:
  7.2 40.3 %copy-start = (bf16[128,16]{0,1:T(8,128)(2,1)S(1)}, bf16[128,16]{0,1:T(8,128)(2,1)}, u32[]{:S(2)}) copy-start(bf16[128,16]{0,1:T(8,128)(2,1)} %param.65) | copy-start | bytes 12292
  7.2 444.4 %reduce-scatter.4.cloned.1.call-start = ((), (), s32[]{:S(2)}) async-start(), calls=%async_computation.1 | async-start | bytes 786432
  8.2 24.4 %collective-permute-start = (bf16[2,2,16,8,128]{4,3,2,1,0:T(8,128)(2,1)S(1)}, bf16[2,2,16,8,128]{4,3,2,1,0:T(8,128)(2,1)S(1)}, u32[]{:S(2)}, u32[]{:S(2)}) collective-permute-start(bf16[2,2,16,8,128]{4,3,2,1,0:T(8,128)(2,1)S(1)} %slice.1486), channel_id=1, source_target_pairs={{0,2},{1,3},{4,6},{5,7},{8,10},{9,11},{12,14},{13,15},{16,18},{17,... | collective-permute-start | bytes 393224 | tf_op jit(solution)/shard_map/ppermute | solution.py:25
  29.6 24.2 %copy-start.50 = (bf16[1024,16]{1,0:T(8,128)(2,1)}, bf16[1024,16]{1,0:T(8,128)(2,1)S(1)}, u32[]{:S(2)}) copy-start(bf16[1024,16]{1,0:T(8,128)(2,1)S(1)} %reshape.1501) | copy-start | bytes 98308
  35.0 2.4 copy-start.13
  35.1 3.8 copy-start.11
  35.1 6.6 %copy-start.9 = (bf16[2,4,16,8,256]{4,3,2,1,0:T(8,128)(2,1)}, bf16[2,4,16,8,256]{4,3,2,1,0:T(8,128)(2,1)S(1)}, u32[]{:S(2)}) copy-start(bf16[2,4,16,8,256]{4,3,2,1,0:T(8,128)(2,1)S(1)} %get-tuple-element.367) | copy-start | bytes 1572868
  35.1 9.1 %copy-start.7 = (bf16[2,4,16,8,256]{4,3,2,1,0:T(8,128)(2,1)}, bf16[2,4,16,8,256]{4,3,2,1,0:T(8,128)(2,1)S(1)}, u32[]{:S(2)}) copy-start(bf16[2,4,16,8,256]{4,3,2,1,0:T(8,128)(2,1)S(1)} %get-tuple-element.364) | copy-start | bytes 1572868
  35.1 9.7 %copy-start.5 = (bf16[2,4,16,8,256]{4,3,2,1,0:T(8,128)(2,1)}, bf16[2,4,16,8,256]{4,3,2,1,0:T(8,128)(2,1)S(1)}, u32[]{:S(2)}) copy-start(bf16[2,4,16,8,256]{4,3,2,1,0:T(8,128)(2,1)S(1)} %get-tuple-element.365) | copy-start | bytes 1572868
  35.1 10.0 %copy-start.3 = (bf16[2,4,16,8,256]{4,3,2,1,0:T(8,128)(2,1)}, bf16[2,4,16,8,256]{4,3,2,1,0:T(8,128)(2,1)S(1)}, u32[]{:S(2)}) copy-start(bf16[2,4,16,8,256]{4,3,2,1,0:T(8,128)(2,1)S(1)} %get-tuple-element.366) | copy-start | bytes 1572868
  35.1 2.6 copy-start.2
  37.2 2.3 copy-start.40
  37.2 2.6 copy-start.38
  37.3 2.8 copy-start.36
  37.3 3.1 copy-start.34
  37.3 3.4 copy-start.32
  37.3 3.7 copy-start.30
  37.3 4.0 copy-start.28
  37.3 4.6 copy-start.42
  37.3 4.6 copy-start.44
  37.3 4.6 copy-start.45
  37.3 4.6 copy-start.46
  37.3 4.6 copy-start.26
  37.4 4.9 %copy-start.24 = (bf16[2,4,16,8,256]{4,3,2,1,0:T(8,128)(2,1)}, bf16[2,4,16,8,256]{4,3,2,1,0:T(8,128)(2,1)S(1)}, u32[]{:S(2)}) copy-start(bf16[2,4,16,8,256]{4,3,2,1,0:T(8,128)(2,1)S(1)} %get-tuple-element.357) | copy-start | bytes 1572868
  37.4 5.2 %copy-start.22 = (bf16[2,4,16,8,256]{4,3,2,1,0:T(8,128)(2,1)}, bf16[2,4,16,8,256]{4,3,2,1,0:T(8,128)(2,1)S(1)}, u32[]{:S(2)}) copy-start(bf16[2,4,16,8,256]{4,3,2,1,0:T(8,128)(2,1)S(1)} %get-tuple-element.358) | copy-start | bytes 1572868
  37.4 5.5 %copy-start.20 = (bf16[2,4,16,8,256]{4,3,2,1,0:T(8,128)(2,1)}, bf16[2,4,16,8,256]{4,3,2,1,0:T(8,128)(2,1)S(1)}, u32[]{:S(2)}) copy-start(bf16[2,4,16,8,256]{4,3,2,1,0:T(8,128)(2,1)S(1)} %get-tuple-element.359) | copy-start | bytes 1572868
  37.4 5.8 %copy-start.18 = (bf16[2,4,16,8,256]{4,3,2,1,0:T(8,128)(2,1)}, bf16[2,4,16,8,256]{4,3,2,1,0:T(8,128)(2,1)S(1)}, u32[]{:S(2)}) copy-start(bf16[2,4,16,8,256]{4,3,2,1,0:T(8,128)(2,1)S(1)} %get-tuple-element.360) | copy-start | bytes 1572868
  37.4 6.2 %copy-start.16 = (bf16[2,4,16,8,256]{4,3,2,1,0:T(8,128)(2,1)}, bf16[2,4,16,8,256]{4,3,2,1,0:T(8,128)(2,1)S(1)}, u32[]{:S(2)}) copy-start(bf16[2,4,16,8,256]{4,3,2,1,0:T(8,128)(2,1)S(1)} %get-tuple-element.361) | copy-start | bytes 1572868
  37.4 6.5 %copy-start.14 = (bf16[2,4,16,8,256]{4,3,2,1,0:T(8,128)(2,1)}, bf16[2,4,16,8,256]{4,3,2,1,0:T(8,128)(2,1)S(1)}, u32[]{:S(2)}) copy-start(bf16[2,4,16,8,256]{4,3,2,1,0:T(8,128)(2,1)S(1)} %get-tuple-element.362) | copy-start | bytes 1572868
  37.4 8.3 %copy-start.48 = (bf16[2,4,16,8,256]{4,3,2,1,0:T(8,128)(2,1)}, bf16[2,4,16,8,256]{4,3,2,1,0:T(8,128)(2,1)S(1)}, u32[]{:S(2)}) copy-start(bf16[2,4,16,8,256]{4,3,2,1,0:T(8,128)(2,1)S(1)} %get-tuple-element.344) | copy-start | bytes 1572868
  46.8 0.7 copy-start.51
  52.1 10.2 %copy-start.12 = (bf16[2,4,16,8,256]{4,3,2,1,0:T(8,128)(2,1)S(1)}, bf16[2,4,16,8,256]{4,3,2,1,0:T(8,128)(2,1)}, u32[]{:S(2)}) copy-start(bf16[2,4,16,8,256]{4,3,2,1,0:T(8,128)(2,1)} %copy-done.11) | copy-start | bytes 1572868
  52.2 358.9 %collective-permute-start.1 = (bf16[2,4,16,128]{3,2,1,0:T(8,128)(2,1)S(1)}, bf16[2,4,16,128]{3,2,1,0:T(8,128)(2,1)S(1)}, u32[]{:S(2)}, u32[]{:S(2)}) collective-permute-start(bf16[2,4,16,128]{3,2,1,0:T(8,128)(2,1)S(1)} %reshape.1498), channel_id=1, source_target_pairs={{0,4},{4,0},{8,12},{12,8},{1,5},{5,1},{9,13},{13,9},{2,6},{6,2},{1... | collective-permute-start | bytes 98312 | tf_op jit(solution)/shard_map/ppermute | solution.py:14
  55.0 7.7 %copy-start.43 = (bf16[2,4,16,8,256]{4,3,2,1,0:T(8,128)(2,1)S(1)}, bf16[2,4,16,8,256]{4,3,2,1,0:T(8,128)(2,1)}, u32[]{:S(2)}) copy-start(bf16[2,4,16,8,256]{4,3,2,1,0:T(8,128)(2,1)} %copy-done.42) | copy-start | bytes 1572868
  55.0 8.1 %copy-start.41 = (bf16[2,4,16,8,256]{4,3,2,1,0:T(8,128)(2,1)S(1)}, bf16[2,4,16,8,256]{4,3,2,1,0:T(8,128)(2,1)}, u32[]{:S(2)}) copy-start(bf16[2,4,16,8,256]{4,3,2,1,0:T(8,128)(2,1)} %copy-done.40) | copy-start | bytes 1572868
  56.5 7.0 %copy-start.39 = (bf16[2,4,16,8,256]{4,3,2,1,0:T(8,128)(2,1)S(1)}, bf16[2,4,16,8,256]{4,3,2,1,0:T(8,128)(2,1)}, u32[]{:S(2)}) copy-start(bf16[2,4,16,8,256]{4,3,2,1,0:T(8,128)(2,1)} %copy-done.38) | copy-start | bytes 1572868
  56.5 7.3 %copy-start.37 = (bf16[2,4,16,8,256]{4,3,2,1,0:T(8,128)(2,1)S(1)}, bf16[2,4,16,8,256]{4,3,2,1,0:T(8,128)(2,1)}, u32[]{:S(2)}) copy-start(bf16[2,4,16,8,256]{4,3,2,1,0:T(8,128)(2,1)} %copy-done.36) | copy-start | bytes 1572868
  58.0 6.2 %copy-start.35 = (bf16[2,4,16,8,256]{4,3,2,1,0:T(8,128)(2,1)S(1)}, bf16[2,4,16,8,256]{4,3,2,1,0:T(8,128)(2,1)}, u32[]{:S(2)}) copy-start(bf16[2,4,16,8,256]{4,3,2,1,0:T(8,128)(2,1)} %copy-done.34) | copy-start | bytes 1572868
  59.4 5.1 %copy-start.33 = (bf16[2,4,16,8,256]{4,3,2,1,0:T(8,128)(2,1)S(1)}, bf16[2,4,16,8,256]{4,3,2,1,0:T(8,128)(2,1)}, u32[]{:S(2)}) copy-start(bf16[2,4,16,8,256]{4,3,2,1,0:T(8,128)(2,1)} %copy-done.32) | copy-start | bytes 1572868
  60.9 4.0 copy-start.31
  62.3 2.9 copy-start.29
  62.7 2.9 copy-start.10
  63.1 2.9 copy-start.27
  63.4 2.9 copy-start.25
  63.8 2.9 copy-start.23
  64.1 2.9 copy-start.21
  64.5 2.8 copy-start.19
  64.9 2.8 copy-start.17
  65.2 2.8 copy-start.15
  65.6 2.8 copy-start.8
  66.3 2.8 copy-start.6
  66.7 2.8 copy-start.4
  67.4 2.8 copy-start.49
  70.5 1.7 copy-start.47
  255.8 160.8 %collective-permute-start.3 = (f32[2,2,16,8,256]{4,3,2,1,0:T(8,128)S(1)}, f32[2,2,16,8,256]{4,3,2,1,0:T(8,128)S(1)}, u32[]{:S(2)}, u32[]{:S(2)}) collective-permute-start(f32[2,2,16,8,256]{4,3,2,1,0:T(8,128)S(1)} %slice.1599), channel_id=1, source_target_pairs={{2,0},{3,1},{6,4},{7,5},{10,8},{11,9},{14,12},{15,13},{18,16},{19,... | collective-permute-start | bytes 1572872 | tf_op jit(solution)/shard_map/ppermute | solution.py:25
  411.1 5.4 %collective-permute-start.2 = (bf16[4,4,16,128]{3,2,1,0:T(8,128)(2,1)S(1)}, bf16[4,4,16,128]{3,2,1,0:T(8,128)(2,1)S(1)}, u32[]{:S(2)}, u32[]{:S(2)}) collective-permute-start(bf16[4,4,16,128]{3,2,1,0:T(8,128)(2,1)S(1)} %maximum_select_fusion.2), channel_id=1, source_target_pairs={{0,8},{4,12},{8,0},{12,4},{1,9},{5,13},{9,1},{13,5},{2,10},{6,14},... | collective-permute-start | bytes 196616 | tf_op jit(solution)/shard_map/ppermute | solution.py:14
  443.4 21.1 %copy-start.1 = (bf16[128,16]{0,1:T(8,128)(2,1)S(1)}, bf16[128,16]{0,1:T(8,128)(2,1)}, u32[]{:S(2)}) copy-start(bf16[128,16]{0,1:T(8,128)(2,1)} %param.65) | copy-start | bytes 12292
Sparse Core Ops, SparseCore 0:
  443.4 8.0 reduce-scatter.3
